TPU v7x, 128 devices: a whole 4x4x4 slice. The times are simulated.
128 devices in a mesh: expert: 32 (over y, z, core), dp: 4 (over x).
Axes of the slice: x: 4, y: 4, z: 4, core: 2. Of those that a mesh axis runs over, the one named last changes fastest.
Arguments:
- activations: bfloat16 [2048, 7168], P(('expert', 'dp')), may hold values from -6 to 6
- cotangent: bfloat16 [2048, 7168], P(('expert', 'dp')), may hold values from -6 to 6
- route_ids: int32 [2048, 8], P(('expert', 'dp')), may hold values from 0 to 31, all different within a row; in each aligned block of 16 rows (0 to 15, 16 to 31, ...) at most 5 rows name the same one
- route_weights: float32 [2048, 8], P(('expert', 'dp')), may hold values from 0.05 to 0.6
- gate_weights: bfloat16 [32, 7168, 1024], P('expert', 'dp'), may hold values from -0.0625 to 0.0625
- up_weights: bfloat16 [32, 7168, 1024], P('expert', 'dp'), may hold values from -0.0625 to 0.0625
- down_weights: bfloat16 [32, 1024, 7168], P('expert', None, 'dp'), may hold values from -0.1875 to 0.1875
Outputs:
- grad_input: bfloat16 [2048, 7168], P(('expert', 'dp'))
- grad_gate: bfloat16 [32, 7168, 1024], P('expert', 'dp')
- grad_up: bfloat16 [32, 7168, 1024], P('expert', 'dp')
- grad_down: bfloat16 [32, 1024, 7168], P('expert', None, 'dp')
Inputs may be any that keep to these rules, and one draw needn't show every extreme that they name: `route_ids`: each token names 8 different experts. Among the routes of one device's 16 tokens, no expert is named more than 5 times, a bound that some block reaches.
All inputs are finite; a program needn't handle non-finite values.
Results may differ from a plain program's by a relative error of at most 0.0064.
Values may be sent and summed in bfloat16 or wider, within the bound.
No kernel may reach another device: no remote copies, remote signals or barrier semaphores. Data moves between devices by JAX's collectives and lax.ppermute only.
A program may use at most 128 MiB of HBM per device.

v0:
```python
import jax
import jax.numpy as jnp
from jax import lax
from jax.sharding import PartitionSpec as P


def swiglu_back(gate, upper, upstream):
    sigma = jax.nn.sigmoid(gate)
    silu_gate = gate * sigma
    activated = (silu_gate * upper).astype(jnp.bfloat16)
    grad_pre = (upstream * upper * sigma * (1.0 + gate * (1.0 - sigma))).astype(jnp.bfloat16)
    grad_lin = (upstream * silu_gate).astype(jnp.bfloat16)
    return (grad_pre, grad_lin, activated)


def contract_rows(left, right):
    return lax.dot_general(
        left, right, (((0,), (0,)), ((), ())), preferred_element_type=jnp.float32
    )


def exchange(parts, num_dp):
    rows, cols = parts.shape
    parts = parts.reshape(num_dp, rows // num_dp, cols)
    me = lax.axis_index("dp")
    summed = lax.dynamic_index_in_dim(parts, me, 0, keepdims=False)
    for shift in range(1, num_dp):
        block = lax.dynamic_index_in_dim(parts, (me + shift) % num_dp, 0, keepdims=False)
        pairs = [(i, (i + shift) % num_dp) for i in range(num_dp)]
        came = lax.ppermute(block.astype(jnp.bfloat16), "dp", pairs)
        summed = summed + came.astype(jnp.float32)
    return summed


def shards(
    activations, cotangent, route_ids, route_weights, gate_weights, up_weights, down_weights
):
    tok_rows, width = activations.shape
    topk = route_ids.shape[1]
    num_dp = lax.axis_size("dp")
    num_exp = lax.axis_size("expert")
    slice_width = gate_weights.shape[1]
    hidden = gate_weights.shape[2]
    capacity = min(tok_rows, 5 * tok_rows * topk // (4 * num_exp))
    flat_ids = route_ids.reshape(-1)
    expert_iota = jnp.arange(num_exp, dtype=jnp.int32)
    onehot = (flat_ids[:, None] == expert_iota[None, :]).astype(jnp.int32)
    before = jnp.cumsum(onehot, axis=0) - onehot
    slot = jnp.sum(before * onehot, axis=1)
    target = (flat_ids * capacity + slot).reshape(tok_rows, topk)
    slot_iota = jnp.arange(num_exp * capacity, dtype=jnp.int32)
    matches = target[:, :, None] == slot_iota[None, None, :]
    placing = jnp.any(matches, axis=1).astype(jnp.bfloat16)
    slot_weight = jnp.sum(jnp.where(matches, route_weights[:, :, None], 0.0), axis=(0, 1))
    by_slice = lambda a: jnp.swapaxes(a.reshape(tok_rows, num_dp, slice_width), 0, 1)
    both = jnp.concatenate([by_slice(activations), by_slice(cotangent)], axis=2)
    slots = placing.T.reshape(num_exp, capacity, tok_rows)
    scale = slot_weight.reshape(num_exp, capacity)
    gate_local = gate_weights[0]
    up_local = up_weights[0]
    down_local = down_weights[0]
    axes = ("dp", "expert")
    split = (capacity + 1) // 2
    bounds = [(0, split), (split, capacity)]
    kept = []
    pieces = []
    for lo, hi in bounds:
        take = hi - lo
        rows = num_exp * take
        pick = jnp.broadcast_to(
            slots[:, lo:hi].reshape(1, rows, tok_rows), (num_dp, rows, tok_rows)
        )
        gathered_rows = lax.dot_general(
            pick, both, (((2,), (1,)), ((0,), (0,))), preferred_element_type=jnp.float32
        )
        weight = jnp.concatenate(
            [
                jnp.ones((rows, slice_width), jnp.float32),
                jnp.broadcast_to(scale[:, lo:hi].reshape(rows, 1), (rows, slice_width)),
            ],
            axis=1,
        )
        flat_both = (gathered_rows * weight[None]).astype(jnp.bfloat16)
        flat_both = flat_both.reshape(num_dp * num_exp, take, 2 * slice_width)
        recv_both = lax.all_to_all(flat_both, axes, split_axis=0, concat_axis=0, tiled=True)
        recv_both = recv_both.reshape(num_exp * num_dp * take, 2 * slice_width)
        act_rows = recv_both[:, :slice_width]
        cot_rows = recv_both[:, slice_width:]
        gate_part = jnp.dot(act_rows, gate_local, preferred_element_type=jnp.float32)
        up_part = jnp.dot(act_rows, up_local, preferred_element_type=jnp.float32)
        back_part = lax.dot_general(
            cot_rows, down_local, (((1,), (1,)), ((), ())), preferred_element_type=jnp.float32
        )
        summed = exchange(jnp.concatenate([gate_part, up_part, back_part], axis=1), num_dp)
        grad_pre, grad_lin, activated = swiglu_back(
            summed[:, :hidden], summed[:, hidden : 2 * hidden], summed[:, 2 * hidden :]
        )
        gathered = lax.all_gather(
            jnp.concatenate([grad_pre, grad_lin, activated], axis=1), "dp", axis=0, tiled=True
        )
        grad_pre = gathered[:, :hidden]
        grad_lin = gathered[:, hidden : 2 * hidden]
        activated = gathered[:, 2 * hidden :]
        rows_back = lax.dot_general(
            grad_pre, gate_local, (((1,), (1,)), ((), ())), preferred_element_type=jnp.float32
        ) + lax.dot_general(
            grad_lin, up_local, (((1,), (1,)), ((), ())), preferred_element_type=jnp.float32
        )
        kept.append((act_rows, cot_rows, grad_pre, grad_lin, activated))
        flat_back = rows_back.astype(jnp.bfloat16).reshape(num_dp * num_exp, take, slice_width)
        arrived = lax.all_to_all(flat_back, axes, split_axis=0, concat_axis=0, tiled=True)
        pieces.append(arrived.reshape(num_dp, num_exp, take, slice_width))
    act_all, cot_all, pre_all, lin_all, activated_all = (
        jnp.concatenate(group, axis=0) for group in zip(*kept)
    )
    grad_gate = contract_rows(act_all, pre_all).astype(jnp.bfloat16)[None]
    grad_up = contract_rows(act_all, lin_all).astype(jnp.bfloat16)[None]
    grad_down = contract_rows(activated_all, cot_all).astype(jnp.bfloat16)[None]
    arrived = jnp.concatenate(pieces, axis=2).reshape(num_dp, num_exp * capacity, slice_width)
    spread = jnp.broadcast_to(placing[None], (num_dp,) + placing.shape)
    grad_slices = lax.dot_general(
        spread, arrived, (((2,), (1,)), ((0,), (0,))), preferred_element_type=jnp.float32
    ).astype(jnp.bfloat16)
    grad_input = jnp.swapaxes(grad_slices, 0, 1).reshape(tok_rows, width)
    return (grad_input, grad_gate, grad_up, grad_down)


def solution(mesh):
    placed = (
        P(("expert", "dp"), None),
        P(("expert", "dp"), None),
        P(("expert", "dp"), None),
        P(("expert", "dp"), None),
        P("expert", "dp", None),
        P("expert", "dp", None),
        P("expert", None, "dp"),
    )
    return jax.shard_map(
        shards,
        mesh=mesh,
        in_specs=placed,
        out_specs=(
            P(("expert", "dp"), None),
            P("expert", "dp", None),
            P("expert", "dp", None),
            P("expert", None, "dp"),
        ),
        check_vma=False,
    )
```

profile of v0, /device:TPU:1, one launch (start us, length us, event | category | flops | bytes accessed | tf_op | source)
XLA Modules:
  0.0 270.5 jit_solution(9096746041630390274)
XLA Ops:
  7.2 0.8 copy.51
  8.1 0.8 copy.57
  8.9 0.2 reduce_window_sum.11
  9.1 0.2 select_reduce_fusion.1
  10.4 0.7 fusion.1
  11.1 1.6 reshape.97
  12.8 11.9 %all-to-all-start.2 = ((bf16[128,2,3584]{2,1,0:T(2,128)(2,1)}), bf16[128,2,3584]{2,1,0:T(2,128)(2,1)}, u32[]{:S(2)}, u32[]{:S(2)}) async-start(bf16[128,2,3584]{2,1,0:T(2,128)(2,1)} %reshape.97), calls=%async_computation.2 | async-start | bytes 3670016 | tf_op jit(solution)/shard_map/all_to_all | solution.py:85
  25.2 0.9 fusion
  26.1 4.0 %reshape.92 = bf16[128,3,3584]{2,1,0:T(4,128)(2,1)} reshape(bf16[4,96,3584]{2,1,0:T(8,128)(2,1)S(1)} %fusion) | data formatting | bytes 5505024 | tf_op jit(solution)/shard_map/reshape | solution.py:84
  30.2 21.8 %all-to-all-done.2 = bf16[128,2,3584]{2,1,0:T(2,128)(2,1)} async-done(((bf16[128,2,3584]{2,1,0:T(2,128)(2,1)}), bf16[128,2,3584]{2,1,0:T(2,128)(2,1)}, u32[]{:S(2)}, u32[]{:S(2)}) %all-to-all-start.2) | async-done | bytes 1835040 | tf_op jit(solution)/shard_map/all_to_all | solution.py:85
  52.0 5.7 %all-to-all-start = ((bf16[128,3,3584]{2,1,0:T(4,128)(2,1)}), bf16[128,3,3584]{2,1,0:T(4,128)(2,1)}, u32[]{:S(2)}, u32[]{:S(2)}) async-start(bf16[128,3,3584]{2,1,0:T(4,128)(2,1)} %reshape.92), calls=%async_computation | async-start | bytes 7340032 | tf_op jit(solution)/shard_map/all_to_all | solution.py:85
  57.8 4.1 %reshape.98 = bf16[256,3584]{1,0:T(8,128)(2,1)S(1)} reshape(bf16[128,2,3584]{2,1,0:T(2,128)(2,1)} %all-to-all-done.2) | data formatting | bytes 3670016 | tf_op jit(solution)/shard_map/reshape | solution.py:86
  61.9 3.8 %fusion.8 = f32[256,1024]{1,0:T(8,128)S(1)} fusion(bf16[1,1792,1024]{2,1,0:T(8,128)(2,1)} %param.12, bf16[256,3584]{1,0:T(8,128)(2,1)S(1)} %reshape.98), kind=kOutput, calls=%fused_computation.14 | convolution fusion | flops 939524096 | bytes 5636096 | tf_op jit(solution)/shard_map/dot_general | solution.py:90
  65.7 1.1 fusion.2
  66.9 0.9 copy-done.11
  67.8 1.1 fusion.16
  68.9 0.2 pad_maximum_fusion.1
  69.1 1.0 fusion.60
  70.1 1.4 collective-permute-start.3
  71.5 1.3 collective-permute-start.5
  72.8 1.7 collective-permute-start.4
  74.5 33.5 %collective-permute-done.3 = bf16[64,3072]{1,0:T(8,128)(2,1)} collective-permute-done((bf16[64,3072]{1,0:T(8,128)(2,1)}, bf16[64,3072]{1,0:T(8,128)(2,1)}, u32[]{:S(2)}, u32[]{:S(2)}) %collective-permute-start.3) | collective-permute-done | bytes 393248 | tf_op jit(solution)/shard_map/ppermute | solution.py:30
  108.0 8.5 %collective-permute-done.4 = bf16[64,3072]{1,0:T(8,128)(2,1)} collective-permute-done((bf16[64,3072]{1,0:T(8,128)(2,1)S(1)}, bf16[64,3072]{1,0:T(8,128)(2,1)}, u32[]{:S(2)}, u32[]{:S(2)}) %collective-permute-start.4) | collective-permute-done | bytes 393248 | tf_op jit(solution)/shard_map/ppermute | solution.py:30
  116.5 1.4 fusion.56
  118.0 0.8 pad_maximum_fusion.8
  118.8 0.2 all-gather.3.cloned.1.call-start
  119.1 5.6 %reshape.93 = bf16[384,3584]{1,0:T(8,128)(2,1)S(1)} reshape(bf16[128,3,3584]{2,1,0:T(4,128)(2,1)} %all-to-all-done) | data formatting | bytes 5505024 | tf_op jit(solution)/shard_map/reshape | solution.py:86
  124.7 3.8 %fusion.12 = f32[384,1024]{1,0:T(8,128)S(1)} fusion(bf16[1,1792,1024]{2,1,0:T(8,128)(2,1)} %param.12, bf16[384,3584]{1,0:T(8,128)(2,1)S(1)} %reshape.93), kind=kOutput, calls=%fused_computation.18 | convolution fusion | flops 1409286144 | bytes 6619136 | tf_op jit(solution)/shard_map/dot_general | solution.py:90
  128.5 1.6 fusion.4
  130.2 0.6 copy-done.12
  130.8 1.7 fusion.20
  132.4 0.5 pad_maximum_fusion
  133.0 0.2 fusion.57
  133.2 0.4 collective-permute-start
  133.6 2.4 collective-permute-start.2
  136.0 21.8 %collective-permute-done = bf16[96,3072]{1,0:T(8,128)(2,1)S(1)} collective-permute-done((bf16[96,3072]{1,0:T(8,128)(2,1)S(1)}, bf16[96,3072]{1,0:T(8,128)(2,1)S(1)}, u32[]{:S(2)}, u32[]{:S(2)}) %collective-permute-start) | collective-permute-done | bytes 589856 | tf_op jit(solution)/shard_map/ppermute | solution.py:30
  157.7 12.9 %collective-permute-done.1 = bf16[96,3072]{1,0:T(8,128)(2,1)S(1)} collective-permute-done((bf16[96,3072]{1,0:T(8,128)(2,1)S(1)}, bf16[96,3072]{1,0:T(8,128)(2,1)S(1)}, u32[]{:S(2)}, u32[]{:S(2)}) %collective-permute-start.1) | collective-permute-done | bytes 589856 | tf_op jit(solution)/shard_map/ppermute | solution.py:30
  170.6 0.3 fusion.54
  170.9 0.2 multiply_convert_fusion.2
  171.2 0.9 pad_maximum_fusion.6
  172.1 2.8 %fusion.87 = (bf16[256,1792]{1,0:T(8,128)(2,1)}, bf16[256,1792]{1,0:T(8,128)(2,1)}) fusion(bf16[256,3584]{1,0:T(8,128)(2,1)} %copy-done), kind=kLoop, calls=%fused_computation.114 | loop fusion | bytes 3670016 | tf_op jit(solution)/shard_map/slice | solution.py:88
  174.9 1.7 fusion.85
  176.6 3.5 %fusion.6 = f32[256,1792]{1,0:T(8,128)S(1)} fusion(bf16[1,1792,1024]{2,1,0:T(8,128)(2,1)} %param.12, bf16[256,3072]{1,0:T(8,128)(2,1)} %all-gather.5.cloned.1.call-done), kind=kOutput, calls=%fused_computation.12 | convolution fusion | flops 939524096 | bytes 6029312 | tf_op jit(solution)/shard_map/dot_general | solution.py:106
  180.1 2.2 fusion.34
  182.3 1.3 reshape.100
  183.6 8.1 %all-to-all-start.3 = ((bf16[128,2,1792]{2,1,0:T(2,128)(2,1)}), bf16[128,2,1792]{2,1,0:T(2,128)(2,1)S(1)}, u32[]{:S(2)}, u32[]{:S(2)}) async-start(bf16[128,2,1792]{2,1,0:T(2,128)(2,1)} %reshape.100), calls=%async_computation.3 | async-start | bytes 1835008 | tf_op jit(solution)/shard_map/all_to_all | solution.py:111
  191.7 22.7 %all-gather.3.cloned.1.call-done = bf16[384,3072]{1,0:T(8,128)(2,1)} async-done(((bf16[96,3072]{1,0:T(8,128)(2,1)}), bf16[384,3072]{1,0:T(8,128)(2,1)}) %all-gather.3.cloned.1.call-update) | async-done | bytes 2359312 | tf_op jit(solution)/shard_map/all_gather | solution.py:98
  214.4 4.1 %fusion.10 = f32[384,1792]{1,0:T(8,128)S(1)} fusion(bf16[1,1792,1024]{2,1,0:T(8,128)(2,1)} %param.12, bf16[384,3072]{1,0:T(8,128)(2,1)} %all-gather.3.cloned.1.call-done), kind=kOutput, calls=%fused_computation.16 | convolution fusion | flops 1409286144 | bytes 7208960 | tf_op jit(solution)/shard_map/dot_general | solution.py:106
  218.4 2.8 %fusion.28 = bf16[384,1792]{1,0:T(8,128)(2,1)S(1)} fusion(f32[384,1792]{1,0:T(8,128)S(1)} %fusion.10, bf16[1,1792,1024]{2,1,0:T(8,128)(2,1)S(1)} %copy-done.14, bf16[384,3072]{1,0:T(8,128)(2,1)} %all-gather.3.cloned.1.call-done), kind=kOutput, calls=%fused_computation.33 | convolution fusion | flops 1410662400 | bytes 8585216 | tf_op jit(solution)/shard_map/dot_general | solution.py:104
  221.3 2.1 reshape.95
  223.3 8.8 %all-to-all-start.1 = ((bf16[128,3,1792]{2,1,0:T(4,128)(2,1)}), bf16[128,3,1792]{2,1,0:T(4,128)(2,1)S(1)}, u32[]{:S(2)}, u32[]{:S(2)}) async-start(bf16[128,3,1792]{2,1,0:T(4,128)(2,1)} %reshape.95), calls=%async_computation.1 | async-start | bytes 3670016 | tf_op jit(solution)/shard_map/all_to_all | solution.py:111
  232.1 1.6 fusion.88
  233.8 1.7 copy.61
  235.4 0.2 fusion.86
  235.7 1.1 copy-done.4
  236.8 0.3 copy-done.6
  237.0 4.5 %fusion.23 = bf16[1,1792,1024]{2,1,0:T(8,128)(2,1)} fusion(bf16[256,1792]{1,0:T(8,128)(2,1)S(1)} %copy-done.6, bf16[384,1792]{1,0:T(8,128)(2,1)S(1)} %copy-done.4, bf16[256,1024]{1,0:T(8,128)(2,1)S(1)} %get-tuple-element.18, bf16[384,1024]{1,0:T(8,128)(2,1)S(1)} %get-tuple-element.13), kind=kOutput, calls=%fused_computation.29 | convolution fusion | flops 2357854208 | bytes 7274496 | tf_op jit(solution)/shard_map/dot_general | solution.py:17
  241.6 4.5 %fusion.22 = bf16[1,1792,1024]{2,1,0:T(8,128)(2,1)} fusion(bf16[256,1792]{1,0:T(8,128)(2,1)S(1)} %copy-done.6, bf16[384,1792]{1,0:T(8,128)(2,1)S(1)} %copy-done.4, bf16[256,1024]{1,0:T(8,128)(2,1)S(1)} %get-tuple-element.19, bf16[384,1024]{1,0:T(8,128)(2,1)S(1)} %get-tuple-element.14), kind=kOutput, calls=%fused_computation.28 | convolution fusion | flops 2357854208 | bytes 7274496 | tf_op jit(solution)/shard_map/dot_general | solution.py:17
  246.1 4.5 %fusion.24 = bf16[1,1024,1792]{2,1,0:T(8,128)(2,1)} fusion(bf16[256,1792]{1,0:T(8,128)(2,1)S(1)} %copy-done.5, bf16[384,1792]{1,0:T(8,128)(2,1)S(1)} %copy-done.3, bf16[256,1024]{1,0:T(8,128)(2,1)S(1)} %get-tuple-element.17, bf16[384,1024]{1,0:T(8,128)(2,1)S(1)} %get-tuple-element.12), kind=kOutput, calls=%fused_computation.30 | convolution fusion | flops 2357854208 | bytes 7274496 | tf_op jit(solution)/shard_map/dot_general | solution.py:17
  250.6 9.1 %all-to-all-done.1 = bf16[128,3,1792]{2,1,0:T(4,128)(2,1)S(1)} async-done(((bf16[128,3,1792]{2,1,0:T(4,128)(2,1)}), bf16[128,3,1792]{2,1,0:T(4,128)(2,1)S(1)}, u32[]{:S(2)}, u32[]{:S(2)}) %all-to-all-start.1) | async-done | bytes 1376288 | tf_op jit(solution)/shard_map/all_to_all | solution.py:111
  259.7 1.3 copy.60
  261.1 1.5 pad_maximum_fusion.2
  262.5 0.4 fusion.41
  263.0 0.7 copy.68
  (59 shorter events, 2.0 us)
Async XLA Ops:
  7.2 3.2 %copy-start.7 = (bf16[16,7168]{1,0:T(8,128)(2,1)S(1)}, bf16[16,7168]{1,0:T(8,128)(2,1)}, u32[]{:S(2)}) copy-start(bf16[16,7168]{1,0:T(8,128)(2,1)} %param.8) | copy-start | bytes 688132
  7.2 3.2 %copy-start.8 = (bf16[16,7168]{1,0:T(8,128)(2,1)S(1)}, bf16[16,7168]{1,0:T(8,128)(2,1)}, u32[]{:S(2)}) copy-start(bf16[16,7168]{1,0:T(8,128)(2,1)} %param.7) | copy-start | bytes 688132
  12.8 39.2 %all-to-all-start.2 = ((bf16[128,2,3584]{2,1,0:T(2,128)(2,1)}), bf16[128,2,3584]{2,1,0:T(2,128)(2,1)}, u32[]{:S(2)}, u32[]{:S(2)}) async-start(bf16[128,2,3584]{2,1,0:T(2,128)(2,1)} %reshape.97), calls=%async_computation.2 | async-start | bytes 3670016 | tf_op jit(solution)/shard_map/all_to_all | solution.py:85
  52.0 67.1 %all-to-all-start = ((bf16[128,3,3584]{2,1,0:T(4,128)(2,1)}), bf16[128,3,3584]{2,1,0:T(4,128)(2,1)}, u32[]{:S(2)}, u32[]{:S(2)}) async-start(bf16[128,3,3584]{2,1,0:T(4,128)(2,1)} %reshape.92), calls=%async_computation | async-start | bytes 7340032 | tf_op jit(solution)/shard_map/all_to_all | solution.py:85
  57.7 118.8 %all-gather.5.cloned.1.call-start = ((), (), s32[]{:S(2)}) async-start(), calls=%async_computation.5 | async-start | bytes 1966080 | tf_op jit(solution)/shard_map/all_gather | solution.py:98
  61.8 5.0 %copy-start = (bf16[256,3584]{1,0:T(8,128)(2,1)}, bf16[256,3584]{1,0:T(8,128)(2,1)S(1)}, u32[]{:S(2)}) copy-start(bf16[256,3584]{1,0:T(8,128)(2,1)S(1)} %reshape.98) | copy-start | bytes 5505028
  61.9 3.9 %copy-start.9 = (bf16[1,1024,1792]{2,1,0:T(8,128)(2,1)S(1)}, bf16[1,1024,1792]{2,1,0:T(8,128)(2,1)}, u32[]{:S(2)}) copy-start(bf16[1,1024,1792]{2,1,0:T(8,128)(2,1)} %param.13) | copy-start | bytes 11010052
  65.7 2.0 copy-start.11
  70.1 37.8 %collective-permute-start.3 = (bf16[64,3072]{1,0:T(8,128)(2,1)}, bf16[64,3072]{1,0:T(8,128)(2,1)}, u32[]{:S(2)}, u32[]{:S(2)}) collective-permute-start(bf16[64,3072]{1,0:T(8,128)(2,1)} %get-tuple-element.7), channel_id=1, source_target_pairs={{0,1},{1,2},{2,3},{3,0},{4,5},{5,6},{6,7},{7,4},{8,9},{9,10},{10,1... | collective-permute-start | bytes 1179656 | tf_op jit(solution)/shard_map/ppermute | solution.py:30
  71.5 36.5 %collective-permute-start.5 = (bf16[64,3072]{1,0:T(8,128)(2,1)}, bf16[64,3072]{1,0:T(8,128)(2,1)}, u32[]{:S(2)}, u32[]{:S(2)}) collective-permute-start(bf16[64,3072]{1,0:T(8,128)(2,1)} %get-tuple-element.8), channel_id=1, source_target_pairs={{0,3},{1,0},{2,1},{3,2},{4,7},{5,4},{6,5},{7,6},{8,11},{9,8},{10,9... | collective-permute-start | bytes 1179656 | tf_op jit(solution)/shard_map/ppermute | solution.py:30
  72.8 43.7 %collective-permute-start.4 = (bf16[64,3072]{1,0:T(8,128)(2,1)S(1)}, bf16[64,3072]{1,0:T(8,128)(2,1)}, u32[]{:S(2)}, u32[]{:S(2)}) collective-permute-start(bf16[64,3072]{1,0:T(8,128)(2,1)S(1)} %get-tuple-element.9), channel_id=1, source_target_pairs={{0,2},{1,3},{2,0},{3,1},{4,6},{5,7},{6,4},{7,5},{8,10},{9,11},{10,... | collective-permute-start | bytes 1179656 | tf_op jit(solution)/shard_map/ppermute | solution.py:30
  118.8 95.5 %all-gather.3.cloned.1.call-start = ((), (), s32[]{:S(2)}) async-start(), calls=%async_computation.4 | async-start | bytes 2949120 | tf_op jit(solution)/shard_map/all_gather | solution.py:98
  124.7 3.8 %copy-start.10 = (bf16[1,1024,1792]{2,1,0:T(8,128)(2,1)S(1)}, bf16[1,1024,1792]{2,1,0:T(8,128)(2,1)}, u32[]{:S(2)}) copy-start(bf16[1,1024,1792]{2,1,0:T(8,128)(2,1)} %param.13) | copy-start | bytes 11010052
  128.5 2.2 copy-start.12
  133.2 24.5 %collective-permute-start = (bf16[96,3072]{1,0:T(8,128)(2,1)S(1)}, bf16[96,3072]{1,0:T(8,128)(2,1)S(1)}, u32[]{:S(2)}, u32[]{:S(2)}) collective-permute-start(bf16[96,3072]{1,0:T(8,128)(2,1)S(1)} %get-tuple-element.4), channel_id=1, source_target_pairs={{0,1},{1,2},{2,3},{3,0},{4,5},{5,6},{6,7},{7,4},{8,9},{9,10},{10,1... | collective-permute-start | bytes 1769480 | tf_op jit(solution)/shard_map/ppermute | solution.py:30
  133.6 24.1 %collective-permute-start.2 = (bf16[96,3072]{1,0:T(8,128)(2,1)S(1)}, bf16[96,3072]{1,0:T(8,128)(2,1)S(1)}, u32[]{:S(2)}, u32[]{:S(2)}) collective-permute-start(bf16[96,3072]{1,0:T(8,128)(2,1)S(1)} %get-tuple-element.5), channel_id=1, source_target_pairs={{0,3},{1,0},{2,1},{3,2},{4,7},{5,4},{6,5},{7,6},{8,11},{9,8},{10,9... | collective-permute-start | bytes 1769480 | tf_op jit(solution)/shard_map/ppermute | solution.py:30
  136.0 34.7 %collective-permute-start.1 = (bf16[96,3072]{1,0:T(8,128)(2,1)S(1)}, bf16[96,3072]{1,0:T(8,128)(2,1)S(1)}, u32[]{:S(2)}, u32[]{:S(2)}) collective-permute-start(bf16[96,3072]{1,0:T(8,128)(2,1)S(1)} %get-tuple-element.6), channel_id=1, source_target_pairs={{0,2},{1,3},{2,0},{3,1},{4,6},{5,7},{6,4},{7,5},{8,10},{9,11},{10,... | collective-permute-start | bytes 1769480 | tf_op jit(solution)/shard_map/ppermute | solution.py:30
  176.6 3.5 %copy-start.13 = (bf16[1,1792,1024]{2,1,0:T(8,128)(2,1)S(1)}, bf16[1,1792,1024]{2,1,0:T(8,128)(2,1)}, u32[]{:S(2)}) copy-start(bf16[1,1792,1024]{2,1,0:T(8,128)(2,1)} %param.11) | copy-start | bytes 11010052
  183.6 39.7 %all-to-all-start.3 = ((bf16[128,2,1792]{2,1,0:T(2,128)(2,1)}), bf16[128,2,1792]{2,1,0:T(2,128)(2,1)S(1)}, u32[]{:S(2)}, u32[]{:S(2)}) async-start(bf16[128,2,1792]{2,1,0:T(2,128)(2,1)} %reshape.100), calls=%async_computation.3 | async-start | bytes 1835008 | tf_op jit(solution)/shard_map/all_to_all | solution.py:111
  214.4 4.1 %copy-start.14 = (bf16[1,1792,1024]{2,1,0:T(8,128)(2,1)S(1)}, bf16[1,1792,1024]{2,1,0:T(8,128)(2,1)}, u32[]{:S(2)}) copy-start(bf16[1,1792,1024]{2,1,0:T(8,128)(2,1)} %param.11) | copy-start | bytes 11010052
  223.3 36.4 %all-to-all-start.1 = ((bf16[128,3,1792]{2,1,0:T(4,128)(2,1)}), bf16[128,3,1792]{2,1,0:T(4,128)(2,1)S(1)}, u32[]{:S(2)}, u32[]{:S(2)}) async-start(bf16[128,3,1792]{2,1,0:T(4,128)(2,1)} %reshape.95), calls=%async_computation.1 | async-start | bytes 3670016 | tf_op jit(solution)/shard_map/all_to_all | solution.py:111
  232.1 3.3 %copy-start.2 = (bf16[384,3072]{1,0:T(8,128)(2,1)S(1)}, bf16[384,3072]{1,0:T(8,128)(2,1)}, u32[]{:S(2)}) copy-start(bf16[384,3072]{1,0:T(8,128)(2,1)} %all-gather.3.cloned.1.call-done) | copy-start | bytes 7077892
  235.4 1.3 copy-start.4
  235.4 1.6 copy-start.6
  241.6 4.5 %copy-start.3 = (bf16[384,1792]{1,0:T(8,128)(2,1)S(1)}, bf16[384,1792]{1,0:T(8,128)(2,1)}, u32[]{:S(2)}) copy-start(bf16[384,1792]{1,0:T(8,128)(2,1)} %get-tuple-element.10) | copy-start | bytes 4128772
  241.6 4.5 %copy-start.5 = (bf16[256,1792]{1,0:T(8,128)(2,1)S(1)}, bf16[256,1792]{1,0:T(8,128)(2,1)}, u32[]{:S(2)}) copy-start(bf16[256,1792]{1,0:T(8,128)(2,1)} %get-tuple-element.15) | copy-start | bytes 2752516
  250.6 10.4 %copy-start.1 = (bf16[4,32,2,1792]{3,0,2,1:T(4,128)(2,1)S(1)}, bf16[4,32,2,1792]{3,0,2,1:T(4,128)(2,1)}, u32[]{:S(2)}) copy-start(bf16[4,32,2,1792]{3,0,2,1:T(4,128)(2,1)} %copy.61) | copy-start | bytes 2752516
Sparse Core Ops, SparseCore 0:
  119.0 33.8 all-gather.4
  172.2 42.1 all-gather.2
where the time goes:
time: 271 us
  waiting for transfers between devices  130 us (48%)
  starting transfers between devices  41.8 us (15%)
  matrix products  41.3 us (15%)
  local copies, waits for them, and re-layouts  35.9 us (13%)
  between operations  14.6 us (5%)
  other arithmetic  6.6 us (2%)
    ppermute x6, waiting for transfers between devices, exchange(): came = lax.ppermute(block.astype(jnp.bfloat16), 'dp', pairs)  76.7 us
    all_gather x2, waiting for transfers between devices, shards(): lax.all_gather(jnp.concatenate([grad_pre, grad_lin, activated], axis=1),...  22.7 us
    all_to_all x2, waiting for transfers between devices, shards(): lax.all_to_all(flat_both, axes, split_axis=0, concat_axis=0, tiled=True)  21.8 us
    all_to_all x2, starting transfers between devices, shards(): lax.all_to_all(flat_both, axes, split_axis=0, concat_axis=0, tiled=True)  17.6 us
    all_to_all x2, starting transfers between devices, shards(): lax.all_to_all(flat_back, axes, split_axis=0, concat_axis=0, tiled=True)  16.9 us
    dot_general x3, matrix products, contract_rows(): lax.dot_general(left, right, (((0,), (0,)), ((), ())), preferred_element_...  13.6 us
    reshape x2, local copies, waits for them, and re-layouts, shards(): recv_both = recv_both.reshape(num_exp * num_dp * take, 2 * slice_width)  9.71 us
    all_to_all x2, waiting for transfers between devices, shards(): lax.all_to_all(flat_back, axes, split_axis=0, concat_axis=0, tiled=True)  9.12 us
  transfers between devices with their start and end apart: 12, of which 7 were waited for; matrix products, arithmetic and copies ran while one was open for 26% of the time, Pallas kernels for 0%

commit v1 on v0

--- a/solution.py
+++ b/solution.py
@@ -95,8 +95,16 @@
         grad_pre, grad_lin, activated = swiglu_back(
             summed[:, :hidden], summed[:, hidden : 2 * hidden], summed[:, 2 * hidden :]
         )
-        gathered = lax.all_gather(
-            jnp.concatenate([grad_pre, grad_lin, activated], axis=1), "dp", axis=0, tiled=True
+        gathered = jnp.concatenate(
+            lax.all_to_all(
+                jnp.stack(
+                    [jnp.concatenate([grad_pre, grad_lin, activated], axis=1)] * lax.axis_size("dp")
+                ),
+                "dp",
+                0,
+                0,
+            ),
+            axis=0,
         )
         grad_pre = gathered[:, :hidden]
         grad_lin = gathered[:, hidden : 2 * hidden]

time: 271 us -> 254 us (0.937)
  waiting for transfers between devices: 130 us -> 113 us
  between operations: 14.6 us -> 1.2 us
  local copies, waits for them, and re-layouts: 35.9 us -> 43.6 us
  starting transfers between devices: 41.8 us -> 48 us
    ppermute x6, waiting for transfers between devices: 76.7 us -> 16.4 us  [exchange(): came = lax.ppermute(block.astype(jnp.bfloat16), 'dp', pairs)]
    all_to_all x0 -> x2, waiting for transfers between devices: none -> 29 us  [shards(): lax.all_to_all(jnp.stack([jnp.concatenate([grad_pre, grad_lin, activated]...]
    all_to_all x2, waiting for transfers between devices: 21.8 us -> 50.2 us  [shards(): lax.all_to_all(flat_both, axes, split_axis=0, concat_axis=0, tiled=True)]
    all_gather x2 -> x0, waiting for transfers between devices: 22.7 us -> none  [shards(): lax.all_gather(jnp.concatenate([grad_pre, grad_lin, activated], axis=1),...]
    all_to_all x0 -> x2, starting transfers between devices: none -> 8.85 us  [shards(): lax.all_to_all(jnp.stack([jnp.concatenate([grad_pre, grad_lin, activated]...]
    all_to_all x2, waiting for transfers between devices: 9.12 us -> 17.5 us  [shards(): lax.all_to_all(flat_back, axes, split_axis=0, concat_axis=0, tiled=True)]
    another operation x0 -> x2, local copies, waits for them, and re-layouts: none -> 3.01 us  [shards(): jnp.stack([jnp.concatenate([grad_pre, grad_lin, activated], axis=1)] * la...]
    unnamed x32 -> x36, local copies, waits for them, and re-layouts: 4.45 us -> 6.24 us
  transfers between devices with their start and end apart: 12 -> 12, of which waited for: 7 -> 8; matrix products, arithmetic and copies ran while one was open for 26% -> 30% of each run, Pallas kernels for 0% -> 0%
where the time goes in v1:
time: 254 us; the launch traced here: 253 us
  waiting for transfers between devices  113 us (44%)
  starting transfers between devices  48 us (19%)
  local copies, waits for them, and re-layouts  43.6 us (17%)
  matrix products  40.3 us (16%)
  other arithmetic  7.01 us (3%)
    all_to_all x2, waiting for transfers between devices, shards(): lax.all_to_all(flat_both, axes, split_axis=0, concat_axis=0, tiled=True)  50.2 us
    all_to_all x2, waiting for transfers between devices, shards(): lax.all_to_all(jnp.stack([jnp.concatenate([grad_pre, grad_lin, activated]...  29 us
    all_to_all x2, starting transfers between devices, shards(): lax.all_to_all(flat_both, axes, split_axis=0, concat_axis=0, tiled=True)  17.6 us
    all_to_all x2, waiting for transfers between devices, shards(): lax.all_to_all(flat_back, axes, split_axis=0, concat_axis=0, tiled=True)  17.5 us
    ppermute x6, waiting for transfers between devices, exchange(): came = lax.ppermute(block.astype(jnp.bfloat16), 'dp', pairs)  16.4 us
    all_to_all x2, starting transfers between devices, shards(): lax.all_to_all(flat_back, axes, split_axis=0, concat_axis=0, tiled=True)  14.5 us
    dot_general x3, matrix products, contract_rows(): lax.dot_general(left, right, (((0,), (0,)), ((), ())), preferred_element_...  13.6 us
    reshape x2, local copies, waits for them, and re-layouts, shards(): recv_both = recv_both.reshape(num_exp * num_dp * take, 2 * slice_width)  9.71 us
  transfers between devices with their start and end apart: 12, of which 8 were waited for; matrix products, arithmetic and copies ran while one was open for 30% of the time, Pallas kernels for 0%

profile of v1, /device:TPU:1, one launch (start us, length us, event | category | flops | bytes accessed | tf_op | source)
XLA Modules:
  0.0 253.3 jit_solution(77656667332491750)
XLA Ops:
  0.7 0.8 copy.51
  1.6 0.8 copy.57
  3.9 0.7 fusion.1
  4.6 1.6 reshape.108
  6.2 11.9 %all-to-all-start.3 = ((bf16[128,2,3584]{2,1,0:T(2,128)(2,1)}), bf16[128,2,3584]{2,1,0:T(2,128)(2,1)}, u32[]{:S(2)}, u32[]{:S(2)}) async-start(bf16[128,2,3584]{2,1,0:T(2,128)(2,1)} %reshape.108), calls=%async_computation.3 | async-start | bytes 3670016 | tf_op jit(solution)/shard_map/all_to_all | solution.py:85
  18.6 0.9 fusion
  19.6 4.0 %reshape.102 = bf16[128,3,3584]{2,1,0:T(4,128)(2,1)} reshape(bf16[4,96,3584]{2,1,0:T(8,128)(2,1)S(1)} %fusion) | data formatting | bytes 5505024 | tf_op jit(solution)/shard_map/reshape | solution.py:84
  23.6 21.9 %all-to-all-done.3 = bf16[128,2,3584]{2,1,0:T(2,128)(2,1)} async-done(((bf16[128,2,3584]{2,1,0:T(2,128)(2,1)}), bf16[128,2,3584]{2,1,0:T(2,128)(2,1)}, u32[]{:S(2)}, u32[]{:S(2)}) %all-to-all-start.3) | async-done | bytes 1835040 | tf_op jit(solution)/shard_map/all_to_all | solution.py:85
  45.5 5.7 %all-to-all-start = ((bf16[128,3,3584]{2,1,0:T(4,128)(2,1)}), bf16[128,3,3584]{2,1,0:T(4,128)(2,1)}, u32[]{:S(2)}, u32[]{:S(2)}) async-start(bf16[128,3,3584]{2,1,0:T(4,128)(2,1)} %reshape.102), calls=%async_computation | async-start | bytes 7340032 | tf_op jit(solution)/shard_map/all_to_all | solution.py:85
  51.2 4.1 %reshape.109 = bf16[256,3584]{1,0:T(8,128)(2,1)S(1)} reshape(bf16[128,2,3584]{2,1,0:T(2,128)(2,1)} %all-to-all-done.3) | data formatting | bytes 3670016 | tf_op jit(solution)/shard_map/reshape | solution.py:86
  55.3 3.8 %fusion.8 = f32[256,1024]{1,0:T(8,128)S(1)} fusion(bf16[1,1792,1024]{2,1,0:T(8,128)(2,1)} %param.12, bf16[256,3584]{1,0:T(8,128)(2,1)S(1)} %reshape.109), kind=kOutput, calls=%fused_computation.14 | convolution fusion | flops 939524096 | bytes 5636096 | tf_op jit(solution)/shard_map/dot_general | solution.py:90
  59.2 1.1 fusion.2
  60.4 0.9 copy-done.13
  61.2 1.2 fusion.16
  62.4 0.3 pad_maximum_fusion.1
  62.8 1.7 copy-done.1
  64.4 1.1 fusion.60
  65.6 1.4 collective-permute-start.3
  66.9 1.3 collective-permute-start.5
  68.2 1.7 collective-permute-start.4
  69.9 28.4 %all-to-all-done = bf16[128,3,3584]{2,1,0:T(4,128)(2,1)} async-done(((bf16[128,3,3584]{2,1,0:T(4,128)(2,1)}), bf16[128,3,3584]{2,1,0:T(4,128)(2,1)}, u32[]{:S(2)}, u32[]{:S(2)}) %all-to-all-start) | async-done | bytes 2752544 | tf_op jit(solution)/shard_map/all_to_all | solution.py:85
  98.3 5.6 %reshape.103 = bf16[384,3584]{1,0:T(8,128)(2,1)S(1)} reshape(bf16[128,3,3584]{2,1,0:T(4,128)(2,1)} %all-to-all-done) | data formatting | bytes 5505024 | tf_op jit(solution)/shard_map/reshape | solution.py:86
  103.9 3.8 %fusion.12 = f32[384,1024]{1,0:T(8,128)S(1)} fusion(bf16[1,1792,1024]{2,1,0:T(8,128)(2,1)} %param.12, bf16[384,3584]{1,0:T(8,128)(2,1)S(1)} %reshape.103), kind=kOutput, calls=%fused_computation.18 | convolution fusion | flops 1409286144 | bytes 6619136 | tf_op jit(solution)/shard_map/dot_general | solution.py:90
  107.7 1.6 fusion.4
  109.4 0.4 copy-done.14
  109.8 1.7 fusion.20
  111.4 0.5 pad_maximum_fusion
  112.0 1.5 fusion.57
  113.5 0.4 collective-permute-start
  113.8 2.3 collective-permute-start.2
  116.2 1.7 fusion.56
  118.0 1.3 stack.5
  119.3 4.4 %all-to-all-start.4 = ((bf16[4,64,3072]{2,1,0:T(8,128)(2,1)}), bf16[4,64,3072]{2,1,0:T(8,128)(2,1)}, u32[]{:S(2)}, u32[]{:S(2)}) async-start(bf16[4,64,3072]{2,1,0:T(8,128)(2,1)} %stack.5), calls=%async_computation.4 | async-start | bytes 3145728 | tf_op jit(solution)/shard_map/all_to_all | solution.py:99
  123.7 4.8 %collective-permute-done = bf16[96,3072]{1,0:T(8,128)(2,1)S(1)} collective-permute-done((bf16[96,3072]{1,0:T(8,128)(2,1)}, bf16[96,3072]{1,0:T(8,128)(2,1)S(1)}, u32[]{:S(2)}, u32[]{:S(2)}) %collective-permute-start) | collective-permute-done | bytes 589856 | tf_op jit(solution)/shard_map/ppermute | solution.py:30
  128.5 11.6 %collective-permute-done.1 = bf16[96,3072]{1,0:T(8,128)(2,1)} collective-permute-done((bf16[96,3072]{1,0:T(8,128)(2,1)}, bf16[96,3072]{1,0:T(8,128)(2,1)}, u32[]{:S(2)}, u32[]{:S(2)}) %collective-permute-start.1) | collective-permute-done | bytes 589856 | tf_op jit(solution)/shard_map/ppermute | solution.py:30
  140.1 1.9 fusion.54
  142.3 14.7 %all-to-all-done.4 = bf16[4,64,3072]{2,1,0:T(8,128)(2,1)} async-done(((bf16[4,64,3072]{2,1,0:T(8,128)(2,1)}), bf16[4,64,3072]{2,1,0:T(8,128)(2,1)}, u32[]{:S(2)}, u32[]{:S(2)}) %all-to-all-start.4) | async-done | bytes 1572896 | tf_op jit(solution)/shard_map/all_to_all | solution.py:99
  157.0 1.7 stack.4
  158.7 4.5 %all-to-all-start.1 = ((bf16[4,96,3072]{2,1,0:T(8,128)(2,1)}), bf16[4,96,3072]{2,1,0:T(8,128)(2,1)}, u32[]{:S(2)}, u32[]{:S(2)}) async-start(bf16[4,96,3072]{2,1,0:T(8,128)(2,1)} %stack.4), calls=%async_computation.1 | async-start | bytes 4718592 | tf_op jit(solution)/shard_map/all_to_all | solution.py:99
  163.2 2.9 %fusion.87 = (bf16[256,1792]{1,0:T(8,128)(2,1)}, bf16[256,1792]{1,0:T(8,128)(2,1)}) fusion(bf16[256,3584]{1,0:T(8,128)(2,1)} %copy-done.2), kind=kLoop, calls=%fused_computation.114 | loop fusion | bytes 3670016 | tf_op jit(solution)/shard_map/slice | solution.py:88
  166.1 1.7 fusion.85
  167.8 1.3 copy-done.12
  169.2 2.4 fusion.6
  171.6 2.2 fusion.34
  173.8 1.3 reshape.112
  175.1 14.3 %all-to-all-done.1 = bf16[4,96,3072]{2,1,0:T(8,128)(2,1)} async-done(((bf16[4,96,3072]{2,1,0:T(8,128)(2,1)}), bf16[4,96,3072]{2,1,0:T(8,128)(2,1)}, u32[]{:S(2)}, u32[]{:S(2)}) %all-to-all-start.1) | async-done | bytes 2359328 | tf_op jit(solution)/shard_map/all_to_all | solution.py:99
  189.3 9.8 %all-to-all-start.5 = ((bf16[128,2,1792]{2,1,0:T(2,128)(2,1)}), bf16[128,2,1792]{2,1,0:T(2,128)(2,1)S(1)}, u32[]{:S(2)}, u32[]{:S(2)}) async-start(bf16[128,2,1792]{2,1,0:T(2,128)(2,1)} %reshape.112), calls=%async_computation.5 | async-start | bytes 1835008 | tf_op jit(solution)/shard_map/all_to_all | solution.py:119
  199.2 4.1 %fusion.10 = f32[384,1792]{1,0:T(8,128)S(1)} fusion(bf16[1,1792,1024]{2,1,0:T(8,128)(2,1)} %param.12, bf16[384,3072]{1,0:T(8,128)(2,1)} %bitcast.11), kind=kOutput, calls=%fused_computation.16 | convolution fusion | flops 1409286144 | bytes 7208960 | tf_op jit(solution)/shard_map/dot_general | solution.py:114
  203.3 2.8 %fusion.28 = bf16[384,1792]{1,0:T(8,128)(2,1)S(1)} fusion(f32[384,1792]{1,0:T(8,128)S(1)} %fusion.10, bf16[1,1792,1024]{2,1,0:T(8,128)(2,1)S(1)} %copy-done.16, bf16[384,3072]{1,0:T(8,128)(2,1)} %bitcast.11), kind=kOutput, calls=%fused_computation.33 | convolution fusion | flops 1410662400 | bytes 8585216 | tf_op jit(solution)/shard_map/dot_general | solution.py:112
  206.1 2.1 reshape.106
  208.2 8.8 %all-to-all-done.5 = bf16[128,2,1792]{2,1,0:T(2,128)(2,1)S(1)} async-done(((bf16[128,2,1792]{2,1,0:T(2,128)(2,1)}), bf16[128,2,1792]{2,1,0:T(2,128)(2,1)S(1)}, u32[]{:S(2)}, u32[]{:S(2)}) %all-to-all-start.5) | async-done | bytes 917536 | tf_op jit(solution)/shard_map/all_to_all | solution.py:119
  217.0 4.6 %all-to-all-start.2 = ((bf16[128,3,1792]{2,1,0:T(4,128)(2,1)}), bf16[128,3,1792]{2,1,0:T(4,128)(2,1)S(1)}, u32[]{:S(2)}, u32[]{:S(2)}) async-start(bf16[128,3,1792]{2,1,0:T(4,128)(2,1)} %reshape.106), calls=%async_computation.2 | async-start | bytes 3670016 | tf_op jit(solution)/shard_map/all_to_all | solution.py:119
  221.7 1.5 fusion.88
  223.1 1.7 copy.61
  224.8 2.0 fusion.86
  226.9 0.3 copy-done.7
  227.1 4.5 %fusion.23 = bf16[1,1792,1024]{2,1,0:T(8,128)(2,1)} fusion(bf16[256,1792]{1,0:T(8,128)(2,1)S(1)} %copy-done.7, bf16[384,1792]{1,0:T(8,128)(2,1)S(1)} %copy-done.5, bf16[256,1024]{1,0:T(8,128)(2,1)S(1)} %get-tuple-element.18, bf16[384,1024]{1,0:T(8,128)(2,1)S(1)} %get-tuple-element.13), kind=kOutput, calls=%fused_computation.29 | convolution fusion | flops 2357854208 | bytes 7274496 | tf_op jit(solution)/shard_map/dot_general | solution.py:17
  231.6 4.5 %fusion.22 = bf16[1,1792,1024]{2,1,0:T(8,128)(2,1)} fusion(bf16[256,1792]{1,0:T(8,128)(2,1)S(1)} %copy-done.7, bf16[384,1792]{1,0:T(8,128)(2,1)S(1)} %copy-done.5, bf16[256,1024]{1,0:T(8,128)(2,1)S(1)} %get-tuple-element.19, bf16[384,1024]{1,0:T(8,128)(2,1)S(1)} %get-tuple-element.14), kind=kOutput, calls=%fused_computation.28 | convolution fusion | flops 2357854208 | bytes 7274496 | tf_op jit(solution)/shard_map/dot_general | solution.py:17
  236.2 4.5 %fusion.24 = bf16[1,1024,1792]{2,1,0:T(8,128)(2,1)} fusion(bf16[256,1792]{1,0:T(8,128)(2,1)S(1)} %copy-done.6, bf16[384,1792]{1,0:T(8,128)(2,1)S(1)} %copy-done.4, bf16[256,1024]{1,0:T(8,128)(2,1)S(1)} %get-tuple-element.17, bf16[384,1024]{1,0:T(8,128)(2,1)S(1)} %get-tuple-element.12), kind=kOutput, calls=%fused_computation.30 | convolution fusion | flops 2357854208 | bytes 7274496 | tf_op jit(solution)/shard_map/dot_general | solution.py:17
  240.7 8.7 %all-to-all-done.2 = bf16[128,3,1792]{2,1,0:T(4,128)(2,1)S(1)} async-done(((bf16[128,3,1792]{2,1,0:T(4,128)(2,1)}), bf16[128,3,1792]{2,1,0:T(4,128)(2,1)S(1)}, u32[]{:S(2)}, u32[]{:S(2)}) %all-to-all-start.2) | async-done | bytes 1376288 | tf_op jit(solution)/shard_map/all_to_all | solution.py:119
  249.4 1.3 copy.60
  250.7 1.5 pad_maximum_fusion.2
  252.2 0.4 fusion.41
  252.6 0.7 copy.68
  (63 shorter events, 2.6 us)
Async XLA Ops:
  0.6 3.2 %copy-start.8 = (bf16[16,7168]{1,0:T(8,128)(2,1)S(1)}, bf16[16,7168]{1,0:T(8,128)(2,1)}, u32[]{:S(2)}) copy-start(bf16[16,7168]{1,0:T(8,128)(2,1)} %param.8) | copy-start | bytes 688132
  0.6 3.2 %copy-start.9 = (bf16[16,7168]{1,0:T(8,128)(2,1)S(1)}, bf16[16,7168]{1,0:T(8,128)(2,1)}, u32[]{:S(2)}) copy-start(bf16[16,7168]{1,0:T(8,128)(2,1)} %param.7) | copy-start | bytes 688132
  6.2 39.2 %all-to-all-start.3 = ((bf16[128,2,3584]{2,1,0:T(2,128)(2,1)}), bf16[128,2,3584]{2,1,0:T(2,128)(2,1)}, u32[]{:S(2)}, u32[]{:S(2)}) async-start(bf16[128,2,3584]{2,1,0:T(2,128)(2,1)} %reshape.108), calls=%async_computation.3 | async-start | bytes 3670016 | tf_op jit(solution)/shard_map/all_to_all | solution.py:85
  45.5 52.8 %all-to-all-start = ((bf16[128,3,3584]{2,1,0:T(4,128)(2,1)}), bf16[128,3,3584]{2,1,0:T(4,128)(2,1)}, u32[]{:S(2)}, u32[]{:S(2)}) async-start(bf16[128,3,3584]{2,1,0:T(4,128)(2,1)} %reshape.102), calls=%async_computation | async-start | bytes 7340032 | tf_op jit(solution)/shard_map/all_to_all | solution.py:85
  55.3 5.0 %copy-start.2 = (bf16[256,3584]{1,0:T(8,128)(2,1)}, bf16[256,3584]{1,0:T(8,128)(2,1)S(1)}, u32[]{:S(2)}) copy-start(bf16[256,3584]{1,0:T(8,128)(2,1)S(1)} %reshape.109) | copy-start | bytes 5505028
  55.3 3.9 %copy-start.10 = (bf16[1,1024,1792]{2,1,0:T(8,128)(2,1)S(1)}, bf16[1,1024,1792]{2,1,0:T(8,128)(2,1)}, u32[]{:S(2)}) copy-start(bf16[1,1024,1792]{2,1,0:T(8,128)(2,1)} %param.13) | copy-start | bytes 11010052
  59.2 2.0 copy-start.13
  62.8 1.7 copy-start.1
  65.6 50.6 %collective-permute-start.3 = (bf16[64,3072]{1,0:T(8,128)(2,1)}, bf16[64,3072]{1,0:T(8,128)(2,1)}, u32[]{:S(2)}, u32[]{:S(2)}) collective-permute-start(bf16[64,3072]{1,0:T(8,128)(2,1)} %get-tuple-element.7), channel_id=1, source_target_pairs={{0,1},{1,2},{2,3},{3,0},{4,5},{5,6},{6,7},{7,4},{8,9},{9,10},{10,1... | collective-permute-start | bytes 1179656 | tf_op jit(solution)/shard_map/ppermute | solution.py:30
  66.9 49.2 %collective-permute-start.5 = (bf16[64,3072]{1,0:T(8,128)(2,1)}, bf16[64,3072]{1,0:T(8,128)(2,1)}, u32[]{:S(2)}, u32[]{:S(2)}) collective-permute-start(bf16[64,3072]{1,0:T(8,128)(2,1)} %get-tuple-element.8), channel_id=1, source_target_pairs={{0,3},{1,0},{2,1},{3,2},{4,7},{5,4},{6,5},{7,6},{8,11},{9,8},{10,9... | collective-permute-start | bytes 1179656 | tf_op jit(solution)/shard_map/ppermute | solution.py:30
  68.2 47.9 %collective-permute-start.4 = (bf16[64,3072]{1,0:T(8,128)(2,1)}, bf16[64,3072]{1,0:T(8,128)(2,1)}, u32[]{:S(2)}, u32[]{:S(2)}) collective-permute-start(bf16[64,3072]{1,0:T(8,128)(2,1)} %get-tuple-element.9), channel_id=1, source_target_pairs={{0,2},{1,3},{2,0},{3,1},{4,6},{5,7},{6,4},{7,5},{8,10},{9,11},{10,... | collective-permute-start | bytes 1179656 | tf_op jit(solution)/shard_map/ppermute | solution.py:30
  103.9 3.8 %copy-start.11 = (bf16[1,1024,1792]{2,1,0:T(8,128)(2,1)S(1)}, bf16[1,1024,1792]{2,1,0:T(8,128)(2,1)}, u32[]{:S(2)}) copy-start(bf16[1,1024,1792]{2,1,0:T(8,128)(2,1)} %param.13) | copy-start | bytes 11010052
  107.7 2.0 copy-start.14
  112.0 5.9 %copy-start = (f32[384,3072]{1,0:T(8,128)}, f32[384,3072]{1,0:T(8,128)S(1)}, u32[]{:S(2)}) copy-start(f32[384,3072]{1,0:T(8,128)S(1)} %pad_maximum_fusion) | copy-start | bytes 14155780
  113.5 15.1 %collective-permute-start = (bf16[96,3072]{1,0:T(8,128)(2,1)}, bf16[96,3072]{1,0:T(8,128)(2,1)S(1)}, u32[]{:S(2)}, u32[]{:S(2)}) collective-permute-start(bf16[96,3072]{1,0:T(8,128)(2,1)} %get-tuple-element.4), channel_id=1, source_target_pairs={{0,1},{1,2},{2,3},{3,0},{4,5},{5,6},{6,7},{7,4},{8,9},{9,10},{10,1... | collective-permute-start | bytes 1769480 | tf_op jit(solution)/shard_map/ppermute | solution.py:30
  113.8 14.7 %collective-permute-start.2 = (bf16[96,3072]{1,0:T(8,128)(2,1)}, bf16[96,3072]{1,0:T(8,128)(2,1)}, u32[]{:S(2)}, u32[]{:S(2)}) collective-permute-start(bf16[96,3072]{1,0:T(8,128)(2,1)} %get-tuple-element.5), channel_id=1, source_target_pairs={{0,3},{1,0},{2,1},{3,2},{4,7},{5,4},{6,5},{7,6},{8,11},{9,8},{10,9... | collective-permute-start | bytes 1769480 | tf_op jit(solution)/shard_map/ppermute | solution.py:30
  116.1 24.0 %collective-permute-start.1 = (bf16[96,3072]{1,0:T(8,128)(2,1)}, bf16[96,3072]{1,0:T(8,128)(2,1)}, u32[]{:S(2)}, u32[]{:S(2)}) collective-permute-start(bf16[96,3072]{1,0:T(8,128)(2,1)} %get-tuple-element.6), channel_id=1, source_target_pairs={{0,2},{1,3},{2,0},{3,1},{4,6},{5,7},{6,4},{7,5},{8,10},{9,11},{10,... | collective-permute-start | bytes 1769480 | tf_op jit(solution)/shard_map/ppermute | solution.py:30
  119.3 37.7 %all-to-all-start.4 = ((bf16[4,64,3072]{2,1,0:T(8,128)(2,1)}), bf16[4,64,3072]{2,1,0:T(8,128)(2,1)}, u32[]{:S(2)}, u32[]{:S(2)}) async-start(bf16[4,64,3072]{2,1,0:T(8,128)(2,1)} %stack.5), calls=%async_computation.4 | async-start | bytes 3145728 | tf_op jit(solution)/shard_map/all_to_all | solution.py:99
  158.7 30.6 %all-to-all-start.1 = ((bf16[4,96,3072]{2,1,0:T(8,128)(2,1)}), bf16[4,96,3072]{2,1,0:T(8,128)(2,1)}, u32[]{:S(2)}, u32[]{:S(2)}) async-start(bf16[4,96,3072]{2,1,0:T(8,128)(2,1)} %stack.4), calls=%async_computation.1 | async-start | bytes 4718592 | tf_op jit(solution)/shard_map/all_to_all | solution.py:99
  166.1 3.0 %copy-start.12 = (bf16[1,1792,1024]{2,1,0:T(8,128)(2,1)S(1)}, bf16[1,1792,1024]{2,1,0:T(8,128)(2,1)}, u32[]{:S(2)}) copy-start(bf16[1,1792,1024]{2,1,0:T(8,128)(2,1)} %param.12) | copy-start | bytes 11010052
  169.2 2.4 copy-start.15
  189.3 27.7 %all-to-all-start.5 = ((bf16[128,2,1792]{2,1,0:T(2,128)(2,1)}), bf16[128,2,1792]{2,1,0:T(2,128)(2,1)S(1)}, u32[]{:S(2)}, u32[]{:S(2)}) async-start(bf16[128,2,1792]{2,1,0:T(2,128)(2,1)} %reshape.112), calls=%async_computation.5 | async-start | bytes 1835008 | tf_op jit(solution)/shard_map/all_to_all | solution.py:119
  199.2 4.1 %copy-start.16 = (bf16[1,1792,1024]{2,1,0:T(8,128)(2,1)S(1)}, bf16[1,1792,1024]{2,1,0:T(8,128)(2,1)}, u32[]{:S(2)}) copy-start(bf16[1,1792,1024]{2,1,0:T(8,128)(2,1)} %param.11) | copy-start | bytes 11010052
  217.0 32.4 %all-to-all-start.2 = ((bf16[128,3,1792]{2,1,0:T(4,128)(2,1)}), bf16[128,3,1792]{2,1,0:T(4,128)(2,1)S(1)}, u32[]{:S(2)}, u32[]{:S(2)}) async-start(bf16[128,3,1792]{2,1,0:T(4,128)(2,1)} %reshape.106), calls=%async_computation.2 | async-start | bytes 3670016 | tf_op jit(solution)/shard_map/all_to_all | solution.py:119
  224.8 2.1 copy-start.5
  224.8 2.3 copy-start.7
  231.6 4.5 %copy-start.4 = (bf16[384,1792]{1,0:T(8,128)(2,1)S(1)}, bf16[384,1792]{1,0:T(8,128)(2,1)}, u32[]{:S(2)}) copy-start(bf16[384,1792]{1,0:T(8,128)(2,1)} %get-tuple-element.10) | copy-start | bytes 4128772
  231.6 4.5 %copy-start.6 = (bf16[256,1792]{1,0:T(8,128)(2,1)S(1)}, bf16[256,1792]{1,0:T(8,128)(2,1)}, u32[]{:S(2)}) copy-start(bf16[256,1792]{1,0:T(8,128)(2,1)} %get-tuple-element.15) | copy-start | bytes 2752516
  240.7 10.0 %copy-start.3 = (bf16[4,32,2,1792]{3,0,2,1:T(4,128)(2,1)S(1)}, bf16[4,32,2,1792]{3,0,2,1:T(4,128)(2,1)}, u32[]{:S(2)}) copy-start(bf16[4,32,2,1792]{3,0,2,1:T(4,128)(2,1)} %copy.61) | copy-start | bytes 2752516
